TPU v7x, 32 devices: a whole 2x2x4 slice. The times are simulated.
32 devices in a mesh: section: 4 (over x, core), sp: 2 (over y), rep: 4 (over z).
Axes of the slice: x: 2, y: 2, z: 4, core: 2. Of those that a mesh axis runs over, the one named last changes fastest.
Arguments:
- tokens: float32 [2, 2, 24, 3072], P('sp', None, 'section', 'rep'), may hold values from -120 to 120
- mod_scale: float32 [3072], replicated, may hold values from -3 to 3
- mod_shift: float32 [3072], replicated, may hold values from -3 to 3
- proj_weight: float32 [64, 3072], replicated, may hold values from -0.109375 to 0.109375
- proj_bias: float32 [64], replicated, may hold values from -3 to 3
- noisy_latent: float32 [2, 4, 48, 16], P(None, 'sp', 'section'), may hold values from -120 to 120
- in_weight: float32 [3, 3, 3, 16, 512], replicated, may hold values from -0.3125 to 0.3125
- in_bias: float32 [512], replicated, may hold values from -3 to 3
- conv_weight: bfloat16 [3, 3, 3, 256, 512], P(None, None, None, 'rep'), may hold values from -0.0546875 to 0.0546875
- conv_bias: float32 [256], P('rep'), may hold values from -3 to 3
- norm_gain: float32 [256], P('rep'), may hold values from 0.25 to 1.75
- norm_bias: float32 [256], P('rep'), may hold values from -3 to 3
Outputs:
- decoded: float32 [8, 96, 512], P('sp', 'section', 'rep')
All inputs are finite; a program needn't handle non-finite values.
Results may differ from a plain program's by a relative error of at most 0.0026.
Values sent between devices are 32-bit elements; how exact they have to be, the bound alone decides.
No kernel may reach another device: no remote copies, remote signals or barrier semaphores. Data moves between devices by JAX's collectives and lax.ppermute only.
A program may use at most 64 MiB of HBM per device.

v0:
```python
import jax
import jax.numpy as jnp
from jax import lax
from jax.sharding import PartitionSpec as P

D = 3072
LC = 16
CO = 256
GROUPS = 32


def with_halo(block, sides, width):
    for axis, dim in sides:
        count = lax.axis_size(axis)
        forward = [(i, i + 1) for i in range(count - 1)]
        backward = [(target, source) for source, target in forward]
        low = lax.ppermute(
            lax.slice_in_dim(block, block.shape[dim] - width, None, axis=dim), axis, forward
        )
        high = lax.ppermute(lax.slice_in_dim(block, 0, width, axis=dim), axis, backward)
        block = jnp.concatenate([low, block, high], axis=dim)
    return block


def valid_conv(volume, kernel, kernel_spec, precision_mode):
    front = jnp.concatenate([volume[:1], volume[:1], volume], axis=0)
    result = lax.conv_general_dilated(
        front[None],
        kernel,
        (1, 1, 1),
        "VALID",
        dimension_numbers=("NDHWC", kernel_spec, "NDHWC"),
        precision=precision_mode,
        preferred_element_type=jnp.float32,
    )
    return result[0]


def per_device(
    tokens,
    mod_scale,
    mod_shift,
    proj_weight,
    proj_bias,
    noisy_latent,
    in_weight,
    in_bias,
    conv_weight,
    conv_bias,
    norm_gain,
    norm_bias,
):
    local_width = tokens.shape[-1]
    scaled_weight = proj_weight * (1.0 + mod_scale)[None, :]
    center_column = jnp.sum(scaled_weight, axis=1)
    shift_column = (
        jnp.dot(
            proj_weight,
            mod_shift,
            precision=lax.Precision.HIGHEST,
            preferred_element_type=jnp.float32,
        )
        + proj_bias
    )
    local_weight = lax.dynamic_slice_in_dim(
        scaled_weight, lax.axis_index("rep") * local_width, local_width, 1
    )
    moved_tokens = lax.all_to_all(tokens, "sp", split_axis=1, concat_axis=0, tiled=True)
    projected = lax.dot_general(
        moved_tokens,
        local_weight,
        (((3,), (1,)), ((), ())),
        precision=lax.Precision.HIGHEST,
        preferred_element_type=jnp.float32,
    )
    projected, first_sums, square_sums = (
        projected,
        jnp.sum(moved_tokens, axis=-1),
        jnp.sum(moved_tokens * moved_tokens, axis=-1),
    )
    projected, first_sums, square_sums = lax.psum((projected, first_sums, square_sums), "rep")
    token_mean = first_sums / D
    token_var = square_sums / D - token_mean * token_mean
    velocity = (
        lax.rsqrt(token_var + 1e-06)[..., None]
        * (projected - token_mean[..., None] * center_column)
        + shift_column
    )
    frames, slab_rows, band_cols = (velocity.shape[0], velocity.shape[1], velocity.shape[2])
    patches = (
        velocity.reshape(frames, slab_rows, band_cols, LC, 2, 2)
        .transpose(0, 1, 4, 2, 5, 3)
        .reshape(frames, 2 * slab_rows, 2 * band_cols, LC)
    )
    clean = noisy_latent - 0.5 * patches
    extended = with_halo(clean, (("section", 2), ("sp", 1)), 2)
    inner_features = valid_conv(extended, in_weight, "DHWIO", lax.Precision.HIGHEST) + in_bias
    latent_rows = 2 * slab_rows
    latent_cols = 2 * band_cols
    row_global = lax.axis_index("sp") * latent_rows - 1 + jnp.arange(latent_rows + 2)
    col_global = lax.axis_index("section") * latent_cols - 1 + jnp.arange(latent_cols + 2)
    row_inside = (row_global >= 0) & (row_global < latent_rows * lax.axis_size("sp"))
    col_inside = (col_global >= 0) & (col_global < latent_cols * lax.axis_size("section"))
    inside = row_inside[None, :, None, None] & col_inside[None, None, :, None]
    features = jnp.where(inside, inner_features, 0.0).astype(jnp.bfloat16)
    upsampled = jnp.repeat(jnp.repeat(features, 2, axis=1), 2, axis=2)[:, 1:-1, 1:-1, :]
    mixed = valid_conv(upsampled, conv_weight, "DHWOI", None) + conv_bias
    group_size = CO // GROUPS
    local_groups = mixed.shape[-1] // group_size
    grouped = mixed.reshape(-1, local_groups, group_size)
    cell_count = grouped.shape[0] * group_size * lax.axis_size("section") * lax.axis_size("sp")
    group_mean = lax.psum(jnp.sum(grouped, axis=(0, 2)), ("section", "sp")) / cell_count
    deviation = grouped - group_mean[None, :, None]
    group_var = (
        lax.psum(jnp.sum(deviation * deviation, axis=(0, 2)), ("section", "sp")) / cell_count
    )
    normed = (
        (grouped - group_mean[None, :, None]) * lax.rsqrt(group_var + 1e-06)[None, :, None]
    ).reshape(mixed.shape)
    activated = jax.nn.silu(normed * norm_gain + norm_bias)
    out_rows, out_cols, out_chan = (activated.shape[1], activated.shape[2], activated.shape[3])
    return activated.transpose(1, 2, 3, 0).reshape(out_rows, out_cols, out_chan * frames)


def solution(mesh):
    return jax.shard_map(
        per_device,
        mesh=mesh,
        in_specs=(
            P("sp", None, "section", "rep"),
            P(),
            P(),
            P(),
            P(),
            P(None, "sp", "section", None),
            P(),
            P(),
            P(None, None, None, "rep", None),
            P("rep"),
            P("rep"),
            P("rep"),
        ),
        out_specs=P("sp", "section", "rep"),
        check_vma=False,
    )
```

profile of v0, /device:TPU:0, one launch (start us, length us, event | category | flops | bytes accessed | tf_op | source)
XLA Modules:
  0.0 79.5 jit_solution(5452324065720546734)
XLA Ops:
  0.0 1.6 %copy.53 = f32[1,2,6,768]{3,0,2,1:T(1,128)} copy(f32[1,2,6,768]{3,1,2,0:T(2,128)} %param.12) | data formatting | bytes 73728 | tf_op args[0]
  1.6 4.2 %all-to-all-start = ((f32[1,2,6,768]{3,0,2,1:T(1,128)}), f32[1,2,6,768]{3,0,2,1:T(1,128)S(1)}, u32[]{:S(2)}, u32[]{:S(2)}) async-start(f32[1,2,6,768]{3,0,2,1:T(1,128)} %copy.53), calls=%async_computation | async-start | bytes 73728 | tf_op jit(solution)/shard_map/all_to_all | solution.py:68
  5.8 0.7 broadcast_add_fusion
  6.5 1.3 %fusion.37 = (f32[64]{0:T(128)S(1)}, f32[64,3072]{1,0:T(8,128)S(1)}) fusion(f32[64,3072]{1,0:T(8,128)} %param.15, f32[3072]{0:T(1024)S(1)} %broadcast_add_fusion), kind=kLoop, calls=%fused_computation.63 | loop fusion | flops 393152 | bytes 1585408 | tf_op jit(solution)/shard_map/reduce_sum | solution.py:55
  7.9 0.7 fusion.11
  8.7 1.1 %all-to-all-done = f32[1,2,6,768]{3,0,2,1:T(1,128)S(1)} async-done(((f32[1,2,6,768]{3,0,2,1:T(1,128)}), f32[1,2,6,768]{3,0,2,1:T(1,128)S(1)}, u32[]{:S(2)}, u32[]{:S(2)}) %all-to-all-start) | async-done | bytes 36896 | tf_op jit(solution)/shard_map/all_to_all | solution.py:68
  9.8 0.2 convolution_bitcast_fusion
  10.1 0.2 multiply_reduce_fusion
  10.3 19.4 %all-reduce = (f32[2,1,6,64]{3,2,0,1:T(8,128)S(1)}, f32[2,1,6]{2,0,1:T(2,128)S(1)}, f32[2,1,6]{2,0,1:T(2,128)S(1)}) all-reduce(f32[2,1,6,64]{3,2,0,1:T(8,128)S(1)} %convolution_bitcast_fusion, f32[2,1,6]{2,0,1:T(2,128)S(1)} %bitcast.85, f32[2,1,6]{2,0,1:T(2,128)S(1)} %bitcast.84), channel_id=1, replica_groups=mesh['section'=4,'sp'=2,'rep'=4] {'rep'}, use_global_device_ids=true, to_apply=%region_4.0 | all-reduce | flops 792 | bytes 6336 | tf_op jit(solution)/shard_map/psum | solution.py:81
  29.9 0.1 copy.57
  30.1 1.3 %collective-permute-start = (f32[2,2,2,16]{3,1,2,0:T(2,128)S(1)}, f32[2,2,2,16]{3,1,2,0:T(2,128)S(1)}, u32[]{:S(2)}, u32[]{:S(2)}) collective-permute-start(f32[2,2,2,16]{3,1,2,0:T(2,128)S(1)} %get-tuple-element.12), channel_id=1, source_target_pairs={{0,8},{8,16},{16,24},{1,9},{9,17},{17,25},{2,10},{10,18},{18,26},{... | collective-permute-start | bytes 1544 | tf_op jit(solution)/shard_map/ppermute | solution.py:17
  31.4 1.3 %collective-permute-start.1 = (f32[2,2,2,16]{3,1,2,0:T(2,128)S(1)}, f32[2,2,2,16]{3,1,2,0:T(2,128)S(1)}, u32[]{:S(2)}, u32[]{:S(2)}) collective-permute-start(f32[2,2,2,16]{3,1,2,0:T(2,128)S(1)} %get-tuple-element.13), channel_id=1, source_target_pairs={{8,0},{16,8},{24,16},{9,1},{17,9},{25,17},{10,2},{18,10},{26,18},{... | collective-permute-start | bytes 1544 | tf_op jit(solution)/shard_map/ppermute | solution.py:20
  32.7 3.5 %collective-permute-done.1 = f32[2,2,2,16]{3,1,2,0:T(2,128)S(1)} collective-permute-done((f32[2,2,2,16]{3,1,2,0:T(2,128)S(1)}, f32[2,2,2,16]{3,1,2,0:T(2,128)S(1)}, u32[]{:S(2)}, u32[]{:S(2)}) %collective-permute-start.1) | collective-permute-done | bytes 544 | tf_op jit(solution)/shard_map/ppermute | solution.py:20
  36.2 1.3 %collective-permute-start.3 = (f32[2,2,16,16]{3,1,2,0:T(2,128)S(1)}, f32[2,2,16,16]{3,1,2,0:T(2,128)S(1)}, u32[]{:S(2)}, u32[]{:S(2)}) collective-permute-start(f32[2,2,16,16]{3,1,2,0:T(2,128)S(1)} %pad_maximum_fusion.4), channel_id=1, source_target_pairs={{4,0},{5,1},{6,2},{7,3},{12,8},{13,9},{14,10},{15,11},{20,16},{21,... | collective-permute-start | bytes 12296 | tf_op jit(solution)/shard_map/ppermute | solution.py:20
  37.5 4.5 %collective-permute-start.2 = (f32[2,2,16,16]{3,1,2,0:T(2,128)S(1)}, f32[2,2,16,16]{3,1,2,0:T(2,128)S(1)}, u32[]{:S(2)}, u32[]{:S(2)}) collective-permute-start(f32[2,2,16,16]{3,1,2,0:T(2,128)S(1)} %pad_maximum_fusion.4), channel_id=1, source_target_pairs={{0,4},{1,5},{2,6},{3,7},{8,12},{9,13},{10,14},{11,15},{16,20},{17,... | collective-permute-start | bytes 12296 | tf_op jit(solution)/shard_map/ppermute | solution.py:17
  42.1 1.5 %collective-permute-done.2 = f32[2,2,16,16]{3,1,2,0:T(2,128)S(1)} collective-permute-done((f32[2,2,16,16]{3,1,2,0:T(2,128)S(1)}, f32[2,2,16,16]{3,1,2,0:T(2,128)S(1)}, u32[]{:S(2)}, u32[]{:S(2)}) %collective-permute-start.2) | collective-permute-done | bytes 4128 | tf_op jit(solution)/shard_map/ppermute | solution.py:17
  43.9 2.8 %convolution_select_fusion = f32[2,4,8,2,512]{4,2,3,1,0:T(8,128)S(1)} fusion(f32[3,3,3,16,512]{4,3,2,1,0:T(8,128)} %param.18, f32[4,6,1,7,2,16]{5,3,4,1,0,2:T(8,128)S(1)} %slice.29, f32[4,6,1,8,2,16]{5,3,4,1,0,2:T(8,128)S(1)} %copy.60, pred[8,2]{0,1:T(4,128)(4,1)S(1)} %copy-done.10), kind=kOutput, calls=%fused_computation.8 | convolution fusion | flops 339841024 | bytes 1192976 | tf_op jit(solution)/shard_map/conv_general_dilated | solution.py:27
  46.7 0.2 copy.61
  46.9 0.1 fusion.19
  47.0 0.1 broadcast_in_dim.23
  47.4 0.2 maximum_bitcast_fusion
  47.6 0.5 copy.68
  48.2 0.3 pad.1.clone
  48.4 0.4 copy.64
  49.0 2.0 %select_reduce_fusion.1 = (f32[64]{0:T(128)S(1)}, f32[2,4,8,4,64]{4,2,3,1,0:T(8,128)S(1)}) fusion(f32[64]{0:T(128)S(1)} %copy-done.5, pred[8,4]{0,1:T(4,128)(4,1)S(1)} %copy-done.9, bf16[3,3,3,64,512]{4,3,2,1,0:T(8,128)(2,1)S(1)} %copy-done, bf16[4,6,1,7,2,512]{5,3,4,1,0,2:T(8,128)(2,1)S(1)} %slice.33, bf16[4,6,1,8,4,512]{5,3,4,1,0,2:T(8,128)(2,1)S(1)} %copy.64), kind=kOutput, calls=%fused_computation.31 | convolution fusion | flops 456589248 | bytes 2966048 | tf_op jit(solution)/shard_map/conv_general_dilated | solution.py:27
  51.1 0.1 reduce_sum.70
  51.2 14.4 %psum.38 = f32[8]{0:T(128)S(1)} all-reduce(f32[8]{0:T(128)S(1)} %reduce_sum.70), channel_id=1, replica_groups=mesh['section'=4,'sp'=2,'rep'=4] {'section','sp'}, use_global_device_ids=true, to_apply=%region_8.9 | all-reduce | flops 8 | bytes 64 | tf_op jit(solution)/shard_map/psum | solution.py:112
  65.8 0.1 select_reduce_fusion
  66.0 0.1 reduce_sum.73
  66.2 12.2 %psum.39 = f32[8]{0:T(128)S(1)} all-reduce(f32[8]{0:T(128)S(1)} %reduce_sum.73), channel_id=1, replica_groups=mesh['section'=4,'sp'=2,'rep'=4] {'section','sp'}, use_global_device_ids=true, to_apply=%region_11.12 | all-reduce | flops 8 | bytes 64 | tf_op jit(solution)/shard_map/psum | solution.py:115
  78.7 0.2 copy.66
  78.8 0.7 copy.67
  (54 shorter events, 1.5 us)
Async XLA Ops:
  0.0 49.0 %copy-start = (bf16[3,3,3,64,512]{4,3,2,1,0:T(8,128)(2,1)S(1)}, bf16[3,3,3,64,512]{4,3,2,1,0:T(8,128)(2,1)}, u32[]{:S(2)}) copy-start(bf16[3,3,3,64,512]{4,3,2,1,0:T(8,128)(2,1)} %param.20) | copy-start | bytes 5308420
  0.0 7.9 %copy-start.1 = (f32[64,3072]{1,0:T(8,128)S(1)}, f32[64,3072]{1,0:T(8,128)}, u32[]{:S(2)}) copy-start(f32[64,3072]{1,0:T(8,128)} %param.15) | copy-start | bytes 2359300
  0.0 7.9 %copy-start.6 = (f32[64]{0:T(128)S(1)}, f32[64]{0:T(128)}, u32[]{:S(2)}) copy-start(f32[64]{0:T(128)} %param.16) | copy-start | bytes 772
  0.0 7.9 %copy-start.3 = (f32[3072]{0:T(1024)S(1)}, f32[3072]{0:T(1024)}, u32[]{:S(2)}) copy-start(f32[3072]{0:T(1024)} %param.14) | copy-start | bytes 36868
  0.0 30.0 %copy-start.2 = (f32[2,2,12,16]{3,1,2,0:T(2,128)S(1)}, f32[2,2,12,16]{3,1,2,0:T(2,128)}, u32[]{:S(2)}) copy-start(f32[2,2,12,16]{3,1,2,0:T(2,128)} %param.17) | copy-start | bytes 9220
  1.6 8.2 %all-to-all-start = ((f32[1,2,6,768]{3,0,2,1:T(1,128)}), f32[1,2,6,768]{3,0,2,1:T(1,128)S(1)}, u32[]{:S(2)}, u32[]{:S(2)}) async-start(f32[1,2,6,768]{3,0,2,1:T(1,128)} %copy.53), calls=%async_computation | async-start | bytes 73728 | tf_op jit(solution)/shard_map/all_to_all | solution.py:68
  7.9 36.0 %copy-start.10 = (pred[8,2]{0,1:T(4,128)(4,1)S(1)}, pred[8,2]{0,1:T(4,128)(4,1)}, u32[]{:S(2)}) copy-start(pred[8,2]{0,1:T(4,128)(4,1)} %constant.62) | copy-start | bytes 52
  30.1 2.6 %collective-permute-start = (f32[2,2,2,16]{3,1,2,0:T(2,128)S(1)}, f32[2,2,2,16]{3,1,2,0:T(2,128)S(1)}, u32[]{:S(2)}, u32[]{:S(2)}) collective-permute-start(f32[2,2,2,16]{3,1,2,0:T(2,128)S(1)} %get-tuple-element.12), channel_id=1, source_target_pairs={{0,8},{8,16},{16,24},{1,9},{9,17},{17,25},{2,10},{10,18},{18,26},{... | collective-permute-start | bytes 1544 | tf_op jit(solution)/shard_map/ppermute | solution.py:17
  31.4 4.8 %collective-permute-start.1 = (f32[2,2,2,16]{3,1,2,0:T(2,128)S(1)}, f32[2,2,2,16]{3,1,2,0:T(2,128)S(1)}, u32[]{:S(2)}, u32[]{:S(2)}) collective-permute-start(f32[2,2,2,16]{3,1,2,0:T(2,128)S(1)} %get-tuple-element.13), channel_id=1, source_target_pairs={{8,0},{16,8},{24,16},{9,1},{17,9},{25,17},{10,2},{18,10},{26,18},{... | collective-permute-start | bytes 1544 | tf_op jit(solution)/shard_map/ppermute | solution.py:20
  36.2 5.9 %collective-permute-start.3 = (f32[2,2,16,16]{3,1,2,0:T(2,128)S(1)}, f32[2,2,16,16]{3,1,2,0:T(2,128)S(1)}, u32[]{:S(2)}, u32[]{:S(2)}) collective-permute-start(f32[2,2,16,16]{3,1,2,0:T(2,128)S(1)} %pad_maximum_fusion.4), channel_id=1, source_target_pairs={{4,0},{5,1},{6,2},{7,3},{12,8},{13,9},{14,10},{15,11},{20,16},{21,... | collective-permute-start | bytes 12296 | tf_op jit(solution)/shard_map/ppermute | solution.py:20
  37.5 6.1 %collective-permute-start.2 = (f32[2,2,16,16]{3,1,2,0:T(2,128)S(1)}, f32[2,2,16,16]{3,1,2,0:T(2,128)S(1)}, u32[]{:S(2)}, u32[]{:S(2)}) collective-permute-start(f32[2,2,16,16]{3,1,2,0:T(2,128)S(1)} %pad_maximum_fusion.4), channel_id=1, source_target_pairs={{0,4},{1,5},{2,6},{3,7},{8,12},{9,13},{10,14},{11,15},{16,20},{17,... | collective-permute-start | bytes 12296 | tf_op jit(solution)/shard_map/ppermute | solution.py:17
  43.8 3.0 %copy-start.4 = (f32[512]{0:T(512)S(1)}, f32[512]{0:T(512)}, u32[]{:S(2)}) copy-start(f32[512]{0:T(512)} %param.19) | copy-start | bytes 6148
  48.1 0.9 %copy-start.5 = (f32[64]{0:T(128)S(1)}, f32[64]{0:T(128)}, u32[]{:S(2)}) copy-start(f32[64]{0:T(128)} %param.21) | copy-start | bytes 772
  48.1 0.9 %copy-start.9 = (pred[8,4]{0,1:T(4,128)(4,1)S(1)}, pred[8,4]{0,1:T(4,128)(4,1)}, u32[]{:S(2)}) copy-start(pred[8,4]{0,1:T(4,128)(4,1)} %constant.61) | copy-start | bytes 100
  49.0 29.6 %copy-start.7 = (f32[64]{0:T(128)S(1)}, f32[64]{0:T(128)}, u32[]{:S(2)}) copy-start(f32[64]{0:T(128)} %param.23) | copy-start | bytes 772
  49.0 29.6 %copy-start.8 = (f32[64]{0:T(128)S(1)}, f32[64]{0:T(128)}, u32[]{:S(2)}) copy-start(f32[64]{0:T(128)} %param.22) | copy-start | bytes 772
where the time goes:
time: 80 us; the launch traced here: 79.5 us
  blocking collectives  46.1 us (58%)
  starting transfers between devices  12.7 us (16%)
  waiting for transfers between devices  6.12 us (8%)
  matrix products  5.79 us (7%)
  local copies, waits for them, and re-layouts  5.24 us (7%)
  other arithmetic  3.28 us (4%)
    psum x1, blocking collectives, per_device(): lax.psum((projected, first_sums, square_sums), 'rep')  19.4 us
    psum x1, blocking collectives, per_device(): lax.psum(jnp.sum(grouped, axis=(0, 2)), ('section', 'sp')) / cell_count  14.4 us
    psum x1, blocking collectives, per_device(): lax.psum(jnp.sum(deviation * deviation, axis=(0, 2)), ('section', 'sp'))  12.2 us
    ppermute x2, starting transfers between devices, with_halo(): lax.ppermute(lax.slice_in_dim(block, block.shape[dim] - width, None, axis...  5.84 us
    conv_general_dilated x2, matrix products, valid_conv(): lax.conv_general_dilated(front[None], kernel, (1, 1, 1), 'VALID', dimensi...  4.83 us
    all_to_all x1, starting transfers between devices, per_device(): lax.all_to_all(tokens, 'sp', split_axis=1, concat_axis=0, tiled=True)  4.24 us
    ppermute x2, waiting for transfers between devices, with_halo(): lax.ppermute(lax.slice_in_dim(block, 0, width, axis=dim), axis, backward)  3.47 us
    ppermute x2, starting transfers between devices, with_halo(): lax.ppermute(lax.slice_in_dim(block, 0, width, axis=dim), axis, backward)  2.58 us
  transfers between devices with their start and end apart: 5, of which 3 were waited for; matrix products, arithmetic and copies ran while one was open for 4% of the time, Pallas kernels for 0%

commit v1 on v0

--- a/solution.py
+++ b/solution.py
@@ -112,7 +112,8 @@
     group_mean = lax.psum(jnp.sum(grouped, axis=(0, 2)), ("section", "sp")) / cell_count
     deviation = grouped - group_mean[None, :, None]
     group_var = (
-        lax.psum(jnp.sum(deviation * deviation, axis=(0, 2)), ("section", "sp")) / cell_count
+        lax.psum(lax.psum(jnp.sum(deviation * deviation, axis=(0, 2)), axis_name="sp"), "section")
+        / cell_count
     )
     normed = (
         (grouped - group_mean[None, :, None]) * lax.rsqrt(group_var + 1e-06)[None, :, None]

time: 80 us -> 79 us (0.988)
  blocking collectives: 46.1 us -> 45 us
    psum x1 -> x2, blocking collectives: 12.2 us -> 11.2 us  [the longest x1 6.29 us: per_device(): lax.psum(lax.psum(jnp.sum(deviation * deviation, axis=(0, 2)), axis_name=...]
where the time goes in v1:
time: 79 us; the launch traced here: 78.5 us
  blocking collectives  45 us (57%)
  starting transfers between devices  12.7 us (16%)
  waiting for transfers between devices  6.12 us (8%)
  matrix products  5.79 us (7%)
  local copies, waits for them, and re-layouts  5.23 us (7%)
  other arithmetic  3.28 us (4%)
    psum x1, blocking collectives, per_device(): lax.psum((projected, first_sums, square_sums), 'rep')  19.4 us
    psum x1, blocking collectives, per_device(): lax.psum(jnp.sum(grouped, axis=(0, 2)), ('section', 'sp')) / cell_count  14.4 us
    psum x1, blocking collectives, per_device(): lax.psum(lax.psum(jnp.sum(deviation * deviation, axis=(0, 2)), axis_name=...  6.29 us
    ppermute x2, starting transfers between devices, with_halo(): lax.ppermute(lax.slice_in_dim(block, block.shape[dim] - width, None, axis...  5.84 us
    psum x1, blocking collectives, per_device(): lax.psum(jnp.sum(deviation * deviation, axis=(0, 2)), axis_name='sp')  4.94 us
    conv_general_dilated x2, matrix products, valid_conv(): lax.conv_general_dilated(front[None], kernel, (1, 1, 1), 'VALID', dimensi...  4.83 us
    all_to_all x1, starting transfers between devices, per_device(): lax.all_to_all(tokens, 'sp', split_axis=1, concat_axis=0, tiled=True)  4.24 us
    ppermute x2, waiting for transfers between devices, with_halo(): lax.ppermute(lax.slice_in_dim(block, 0, width, axis=dim), axis, backward)  3.47 us
  transfers between devices with their start and end apart: 5, of which 3 were waited for; matrix products, arithmetic and copies ran while one was open for 4% of the time, Pallas kernels for 0%

profile of v1, /device:TPU:0, one launch (start us, length us, event | category | flops | bytes accessed | tf_op | source)
XLA Modules:
  0.0 78.5 jit_solution(6929237799358188305)
XLA Ops:
  0.0 1.6 %copy.53 = f32[1,2,6,768]{3,0,2,1:T(1,128)} copy(f32[1,2,6,768]{3,1,2,0:T(2,128)} %param.12) | data formatting | bytes 73728 | tf_op args[0]
  1.6 4.2 %all-to-all-start = ((f32[1,2,6,768]{3,0,2,1:T(1,128)}), f32[1,2,6,768]{3,0,2,1:T(1,128)S(1)}, u32[]{:S(2)}, u32[]{:S(2)}) async-start(f32[1,2,6,768]{3,0,2,1:T(1,128)} %copy.53), calls=%async_computation | async-start | bytes 73728 | tf_op jit(solution)/shard_map/all_to_all | solution.py:68
  5.8 0.7 broadcast_add_fusion
  6.5 1.3 %fusion.37 = (f32[64]{0:T(128)S(1)}, f32[64,3072]{1,0:T(8,128)S(1)}) fusion(f32[64,3072]{1,0:T(8,128)} %param.15, f32[3072]{0:T(1024)S(1)} %broadcast_add_fusion), kind=kLoop, calls=%fused_computation.63 | loop fusion | flops 393152 | bytes 1585408 | tf_op jit(solution)/shard_map/reduce_sum | solution.py:55
  7.9 0.7 fusion.11
  8.7 1.1 %all-to-all-done = f32[1,2,6,768]{3,0,2,1:T(1,128)S(1)} async-done(((f32[1,2,6,768]{3,0,2,1:T(1,128)}), f32[1,2,6,768]{3,0,2,1:T(1,128)S(1)}, u32[]{:S(2)}, u32[]{:S(2)}) %all-to-all-start) | async-done | bytes 36896 | tf_op jit(solution)/shard_map/all_to_all | solution.py:68
  9.8 0.2 convolution_bitcast_fusion
  10.1 0.2 multiply_reduce_fusion
  10.3 19.4 %all-reduce = (f32[2,1,6,64]{3,2,0,1:T(8,128)S(1)}, f32[2,1,6]{2,0,1:T(2,128)S(1)}, f32[2,1,6]{2,0,1:T(2,128)S(1)}) all-reduce(f32[2,1,6,64]{3,2,0,1:T(8,128)S(1)} %convolution_bitcast_fusion, f32[2,1,6]{2,0,1:T(2,128)S(1)} %bitcast.85, f32[2,1,6]{2,0,1:T(2,128)S(1)} %bitcast.84), channel_id=1, replica_groups=mesh['section'=4,'sp'=2,'rep'=4] {'rep'}, use_global_device_ids=true, to_apply=%region_4.0 | all-reduce | flops 792 | bytes 6336 | tf_op jit(solution)/shard_map/psum | solution.py:81
  29.9 0.1 copy.57
  30.1 1.3 %collective-permute-start = (f32[2,2,2,16]{3,1,2,0:T(2,128)S(1)}, f32[2,2,2,16]{3,1,2,0:T(2,128)S(1)}, u32[]{:S(2)}, u32[]{:S(2)}) collective-permute-start(f32[2,2,2,16]{3,1,2,0:T(2,128)S(1)} %get-tuple-element.12), channel_id=1, source_target_pairs={{0,8},{8,16},{16,24},{1,9},{9,17},{17,25},{2,10},{10,18},{18,26},{... | collective-permute-start | bytes 1544 | tf_op jit(solution)/shard_map/ppermute | solution.py:17
  31.4 1.3 %collective-permute-start.1 = (f32[2,2,2,16]{3,1,2,0:T(2,128)S(1)}, f32[2,2,2,16]{3,1,2,0:T(2,128)S(1)}, u32[]{:S(2)}, u32[]{:S(2)}) collective-permute-start(f32[2,2,2,16]{3,1,2,0:T(2,128)S(1)} %get-tuple-element.13), channel_id=1, source_target_pairs={{8,0},{16,8},{24,16},{9,1},{17,9},{25,17},{10,2},{18,10},{26,18},{... | collective-permute-start | bytes 1544 | tf_op jit(solution)/shard_map/ppermute | solution.py:20
  32.7 3.5 %collective-permute-done.1 = f32[2,2,2,16]{3,1,2,0:T(2,128)S(1)} collective-permute-done((f32[2,2,2,16]{3,1,2,0:T(2,128)S(1)}, f32[2,2,2,16]{3,1,2,0:T(2,128)S(1)}, u32[]{:S(2)}, u32[]{:S(2)}) %collective-permute-start.1) | collective-permute-done | bytes 544 | tf_op jit(solution)/shard_map/ppermute | solution.py:20
  36.2 1.3 %collective-permute-start.3 = (f32[2,2,16,16]{3,1,2,0:T(2,128)S(1)}, f32[2,2,16,16]{3,1,2,0:T(2,128)S(1)}, u32[]{:S(2)}, u32[]{:S(2)}) collective-permute-start(f32[2,2,16,16]{3,1,2,0:T(2,128)S(1)} %pad_maximum_fusion.4), channel_id=1, source_target_pairs={{4,0},{5,1},{6,2},{7,3},{12,8},{13,9},{14,10},{15,11},{20,16},{21,... | collective-permute-start | bytes 12296 | tf_op jit(solution)/shard_map/ppermute | solution.py:20
  37.5 4.5 %collective-permute-start.2 = (f32[2,2,16,16]{3,1,2,0:T(2,128)S(1)}, f32[2,2,16,16]{3,1,2,0:T(2,128)S(1)}, u32[]{:S(2)}, u32[]{:S(2)}) collective-permute-start(f32[2,2,16,16]{3,1,2,0:T(2,128)S(1)} %pad_maximum_fusion.4), channel_id=1, source_target_pairs={{0,4},{1,5},{2,6},{3,7},{8,12},{9,13},{10,14},{11,15},{16,20},{17,... | collective-permute-start | bytes 12296 | tf_op jit(solution)/shard_map/ppermute | solution.py:17
  42.1 1.5 %collective-permute-done.2 = f32[2,2,16,16]{3,1,2,0:T(2,128)S(1)} collective-permute-done((f32[2,2,16,16]{3,1,2,0:T(2,128)S(1)}, f32[2,2,16,16]{3,1,2,0:T(2,128)S(1)}, u32[]{:S(2)}, u32[]{:S(2)}) %collective-permute-start.2) | collective-permute-done | bytes 4128 | tf_op jit(solution)/shard_map/ppermute | solution.py:17
  43.9 2.8 %convolution_select_fusion = f32[2,4,8,2,512]{4,2,3,1,0:T(8,128)S(1)} fusion(f32[3,3,3,16,512]{4,3,2,1,0:T(8,128)} %param.18, f32[4,6,1,7,2,16]{5,3,4,1,0,2:T(8,128)S(1)} %slice.29, f32[4,6,1,8,2,16]{5,3,4,1,0,2:T(8,128)S(1)} %copy.60, pred[8,2]{0,1:T(4,128)(4,1)S(1)} %copy-done.10), kind=kOutput, calls=%fused_computation.8 | convolution fusion | flops 339841024 | bytes 1192976 | tf_op jit(solution)/shard_map/conv_general_dilated | solution.py:27
  46.7 0.2 copy.61
  47.0 0.1 broadcast_in_dim.23
  47.4 0.2 maximum_bitcast_fusion
  47.6 0.5 copy.68
  48.2 0.3 pad.1.clone
  48.4 0.4 copy.64
  49.0 2.0 %select_reduce_fusion.1 = (f32[64]{0:T(128)S(1)}, f32[2,4,8,4,64]{4,2,3,1,0:T(8,128)S(1)}) fusion(f32[64]{0:T(128)S(1)} %copy-done.5, pred[8,4]{0,1:T(4,128)(4,1)S(1)} %copy-done.9, bf16[3,3,3,64,512]{4,3,2,1,0:T(8,128)(2,1)S(1)} %copy-done, bf16[4,6,1,7,2,512]{5,3,4,1,0,2:T(8,128)(2,1)S(1)} %slice.33, bf16[4,6,1,8,4,512]{5,3,4,1,0,2:T(8,128)(2,1)S(1)} %copy.64), kind=kOutput, calls=%fused_computation.31 | convolution fusion | flops 456589248 | bytes 2966048 | tf_op jit(solution)/shard_map/conv_general_dilated | solution.py:27
  51.1 0.1 reduce_sum.70
  51.2 14.4 %psum.45 = f32[8]{0:T(128)S(1)} all-reduce(f32[8]{0:T(128)S(1)} %reduce_sum.70), channel_id=1, replica_groups=mesh['section'=4,'sp'=2,'rep'=4] {'section','sp'}, use_global_device_ids=true, to_apply=%region_8.9 | all-reduce | flops 8 | bytes 64 | tf_op jit(solution)/shard_map/psum | solution.py:112
  65.8 0.1 select_reduce_fusion
  66.0 0.1 reduce_sum.73
  66.1 4.9 %psum.46 = f32[8]{0:T(128)S(1)} all-reduce(f32[8]{0:T(128)S(1)} %reduce_sum.73), channel_id=1, replica_groups=mesh['section'=4,'sp'=2,'rep'=4] {'sp'}, use_global_device_ids=true, to_apply=%region_11.12 | all-reduce | flops 8 | bytes 64 | tf_op jit(solution)/shard_map/psum | solution.py:115
  71.1 6.3 %psum.47 = f32[8]{0:T(128)S(1)} all-reduce(f32[8]{0:T(128)S(1)} %psum.46), channel_id=1, replica_groups=mesh['section'=4,'sp'=2,'rep'=4] {'section'}, use_global_device_ids=true, to_apply=%region_12.13 | all-reduce | flops 8 | bytes 64 | tf_op jit(solution)/shard_map/psum | solution.py:115
  77.6 0.2 copy.66
  77.8 0.7 copy.67
  (55 shorter events, 1.6 us)
Async XLA Ops:
  0.0 49.0 %copy-start = (bf16[3,3,3,64,512]{4,3,2,1,0:T(8,128)(2,1)S(1)}, bf16[3,3,3,64,512]{4,3,2,1,0:T(8,128)(2,1)}, u32[]{:S(2)}) copy-start(bf16[3,3,3,64,512]{4,3,2,1,0:T(8,128)(2,1)} %param.20) | copy-start | bytes 5308420
  0.0 7.9 %copy-start.1 = (f32[64,3072]{1,0:T(8,128)S(1)}, f32[64,3072]{1,0:T(8,128)}, u32[]{:S(2)}) copy-start(f32[64,3072]{1,0:T(8,128)} %param.15) | copy-start | bytes 2359300
  0.0 7.9 %copy-start.6 = (f32[64]{0:T(128)S(1)}, f32[64]{0:T(128)}, u32[]{:S(2)}) copy-start(f32[64]{0:T(128)} %param.16) | copy-start | bytes 772
  0.0 7.9 %copy-start.3 = (f32[3072]{0:T(1024)S(1)}, f32[3072]{0:T(1024)}, u32[]{:S(2)}) copy-start(f32[3072]{0:T(1024)} %param.14) | copy-start | bytes 36868
  0.0 30.0 %copy-start.2 = (f32[2,2,12,16]{3,1,2,0:T(2,128)S(1)}, f32[2,2,12,16]{3,1,2,0:T(2,128)}, u32[]{:S(2)}) copy-start(f32[2,2,12,16]{3,1,2,0:T(2,128)} %param.17) | copy-start | bytes 9220
  1.6 8.2 %all-to-all-start = ((f32[1,2,6,768]{3,0,2,1:T(1,128)}), f32[1,2,6,768]{3,0,2,1:T(1,128)S(1)}, u32[]{:S(2)}, u32[]{:S(2)}) async-start(f32[1,2,6,768]{3,0,2,1:T(1,128)} %copy.53), calls=%async_computation | async-start | bytes 73728 | tf_op jit(solution)/shard_map/all_to_all | solution.py:68
  7.9 36.0 %copy-start.10 = (pred[8,2]{0,1:T(4,128)(4,1)S(1)}, pred[8,2]{0,1:T(4,128)(4,1)}, u32[]{:S(2)}) copy-start(pred[8,2]{0,1:T(4,128)(4,1)} %constant.62) | copy-start | bytes 52
  30.1 2.6 %collective-permute-start = (f32[2,2,2,16]{3,1,2,0:T(2,128)S(1)}, f32[2,2,2,16]{3,1,2,0:T(2,128)S(1)}, u32[]{:S(2)}, u32[]{:S(2)}) collective-permute-start(f32[2,2,2,16]{3,1,2,0:T(2,128)S(1)} %get-tuple-element.12), channel_id=1, source_target_pairs={{0,8},{8,16},{16,24},{1,9},{9,17},{17,25},{2,10},{10,18},{18,26},{... | collective-permute-start | bytes 1544 | tf_op jit(solution)/shard_map/ppermute | solution.py:17
  31.4 4.8 %collective-permute-start.1 = (f32[2,2,2,16]{3,1,2,0:T(2,128)S(1)}, f32[2,2,2,16]{3,1,2,0:T(2,128)S(1)}, u32[]{:S(2)}, u32[]{:S(2)}) collective-permute-start(f32[2,2,2,16]{3,1,2,0:T(2,128)S(1)} %get-tuple-element.13), channel_id=1, source_target_pairs={{8,0},{16,8},{24,16},{9,1},{17,9},{25,17},{10,2},{18,10},{26,18},{... | collective-permute-start | bytes 1544 | tf_op jit(solution)/shard_map/ppermute | solution.py:20
  36.2 5.9 %collective-permute-start.3 = (f32[2,2,16,16]{3,1,2,0:T(2,128)S(1)}, f32[2,2,16,16]{3,1,2,0:T(2,128)S(1)}, u32[]{:S(2)}, u32[]{:S(2)}) collective-permute-start(f32[2,2,16,16]{3,1,2,0:T(2,128)S(1)} %pad_maximum_fusion.4), channel_id=1, source_target_pairs={{4,0},{5,1},{6,2},{7,3},{12,8},{13,9},{14,10},{15,11},{20,16},{21,... | collective-permute-start | bytes 12296 | tf_op jit(solution)/shard_map/ppermute | solution.py:20
  37.5 6.1 %collective-permute-start.2 = (f32[2,2,16,16]{3,1,2,0:T(2,128)S(1)}, f32[2,2,16,16]{3,1,2,0:T(2,128)S(1)}, u32[]{:S(2)}, u32[]{:S(2)}) collective-permute-start(f32[2,2,16,16]{3,1,2,0:T(2,128)S(1)} %pad_maximum_fusion.4), channel_id=1, source_target_pairs={{0,4},{1,5},{2,6},{3,7},{8,12},{9,13},{10,14},{11,15},{16,20},{17,... | collective-permute-start | bytes 12296 | tf_op jit(solution)/shard_map/ppermute | solution.py:17
  43.8 3.0 %copy-start.4 = (f32[512]{0:T(512)S(1)}, f32[512]{0:T(512)}, u32[]{:S(2)}) copy-start(f32[512]{0:T(512)} %param.19) | copy-start | bytes 6148
  48.1 0.9 %copy-start.5 = (f32[64]{0:T(128)S(1)}, f32[64]{0:T(128)}, u32[]{:S(2)}) copy-start(f32[64]{0:T(128)} %param.21) | copy-start | bytes 772
  48.1 0.9 %copy-start.9 = (pred[8,4]{0,1:T(4,128)(4,1)S(1)}, pred[8,4]{0,1:T(4,128)(4,1)}, u32[]{:S(2)}) copy-start(pred[8,4]{0,1:T(4,128)(4,1)} %constant.61) | copy-start | bytes 100
  49.0 28.6 %copy-start.7 = (f32[64]{0:T(128)S(1)}, f32[64]{0:T(128)}, u32[]{:S(2)}) copy-start(f32[64]{0:T(128)} %param.23) | copy-start | bytes 772
  49.0 28.5 %copy-start.8 = (f32[64]{0:T(128)S(1)}, f32[64]{0:T(128)}, u32[]{:S(2)}) copy-start(f32[64]{0:T(128)} %param.22) | copy-start | bytes 772
